TPU v7x, 256 devices: a whole 4x4x8 slice. The times are simulated.
256 devices in a mesh: lat: 16 (over z_hi, y, core), lon: 16 (over x, z_lo).
Axes of the slice: x: 4, y: 4, z: 8 (z_hi: 2, z_lo: 4; z = z_hi * 4 + z_lo), core: 2. Of those that a mesh axis runs over, the one named last changes fastest.
Arguments:
- forward_state: float32 [256, 32768], P(None, ('lat', 'lon')), may hold values from -6 to 6
- adjoint_state: float32 [256, 32768], P(None, ('lat', 'lon')), may hold values from -6 to 6
- inc_forward: float32 [4, 256, 32768], P(None, None, ('lat', 'lon')), may hold values from -6 to 6
- inc_adjoint: float32 [4, 256, 32768], P(None, None, ('lat', 'lon')), may hold values from -6 to 6
- bulk_modulus: float32 [32768], P(('lat', 'lon')), may hold values from 0.5 to 2
- inverse_size: float32 [32768], P(('lat', 'lon')), may hold values from 0.7 to 1.4
- face_codes: int32 [4, 32768], P(None, ('lat', 'lon')), may hold values from 0 to 7
- block_map: int32 [32768], P(('lat', 'lon')), may hold values from 0 to 255
- probe_dirs: float32 [4, 256], P(None, ('lat', 'lon')), may hold values from -6 to 6
Outputs:
- new_forward: float32 [4, 256, 32768], P(None, None, ('lat', 'lon'))
- new_adjoint: float32 [4, 256, 32768], P(None, None, ('lat', 'lon'))
- hess_vec: float32 [4, 256], P(None, ('lat', 'lon'))
All inputs are finite; a program needn't handle non-finite values.
Results may differ from a plain program's by a relative error of at most 0.00013.
Values sent between devices are 32-bit elements; how exact they have to be, the bound alone decides.
No kernel may reach another device: no remote copies, remote signals or barrier semaphores. Data moves between devices by JAX's collectives and lax.ppermute only.
A program may use at most 64 MiB of HBM per device.

v0:
```python
import jax
import jax.numpy as jnp
import numpy as np
from jax import lax
from jax.sharding import PartitionSpec as P

TIME_STEP = 0.05
PENALTY = 1.0
LIFT_FACTOR = 6.0


def shifted(block, axis, distance):
    devices = range(lax.axis_size(axis))
    route = [(i - distance, i) for i in devices if i - distance in devices]
    return lax.ppermute(block, axis, route)


def from_behind(value, axis, steps):
    count = lax.axis_size(axis)
    pairs = [(source, (source + steps) % count) for source in range(count)]
    return lax.ppermute(value, axis, pairs)


def node_tables():
    spread = 1.0 / np.sqrt(5.0)
    points = np.array([-1.0, -spread, spread, 1.0])
    weights = np.array([1.0, 5.0, 5.0, 1.0]) / 6.0
    products = np.array(
        [np.prod([points[j] - points[k] for k in range(4) if k != j]) for j in range(4)]
    )
    derivative = np.zeros((4, 4))
    for i in range(4):
        for j in range(4):
            if i != j:
                derivative[i, j] = products[i] / products[j] / (points[i] - points[j])
        derivative[i, i] = np.sum([1.0 / (points[i] - points[k]) for k in range(4) if k != i])
    identity = np.eye(4)
    directional = [
        np.kron(derivative, np.kron(identity, identity)),
        np.kron(identity, np.kron(derivative, identity)),
        np.kron(identity, np.kron(identity, derivative)),
    ]
    coupling = np.zeros((256, 256))
    for d in range(3):
        coupling[64 * (d + 1) : 64 * (d + 2), 0:64] = directional[d].T
        coupling[0:64, 64 * (d + 1) : 64 * (d + 2)] = directional[d].T
    selects = np.zeros((256, 192))
    for f in range(6):
        d = f // 2
        for u in range(4):
            for v in range(4):
                position = [u, v]
                position.insert(d, 3 * (f % 2))
                node_id = 16 * position[0] + 4 * position[1] + position[2]
                selects[node_id, 32 * f + 4 * u + v] = 1.0
                selects[64 * (d + 1) + node_id, 32 * f + 16 + 4 * u + v] = 1.0
    orient = np.zeros((8, 32), np.int32)
    for q in range(8):
        for u in range(4):
            for v in range(4):
                source_u, source_v = (v, u) if q & 1 else (u, v)
                if q & 2:
                    source_u = 3 - source_u
                if q & 4:
                    source_v = 3 - source_v
                orient[q, 4 * u + v] = 4 * source_u + source_v
                orient[q, 16 + 4 * u + v] = 16 + 4 * source_u + source_v
    quadrature = np.kron(weights, np.kron(weights, weights))
    return (
        jnp.asarray(coupling, dtype=jnp.float32),
        jnp.asarray(selects, dtype=jnp.float32),
        orient,
        jnp.asarray(quadrature, dtype=jnp.float32),
    )


def volume_rate(states, coupling, bulk_modulus, inverse_size):
    mixed = jnp.einsum("cd,scr->sdr", coupling, states, precision=lax.Precision.HIGHEST)
    channel = lax.broadcasted_iota(jnp.int32, (256, 1), 0)
    factor = jnp.where(
        channel < 64, -(bulk_modulus * inverse_size)[None, :], -inverse_size[None, :]
    )
    return mixed * factor[None]


def face_term(own_trace, neighbour, bulk_modulus, inverse_size, normal_sign):
    jump_pressure = neighbour[:, :16] - own_trace[:, :16]
    jump_velocity = neighbour[:, 16:] - own_trace[:, 16:]
    modulus = bulk_modulus[None, None, :]
    lift_scale = LIFT_FACTOR * inverse_size[None, None, :]
    on_pressure = lift_scale * (
        -modulus * normal_sign * 0.5 * jump_velocity + 0.5 * PENALTY * jump_pressure
    )
    on_velocity = lift_scale * (-normal_sign * 0.5 * jump_pressure + 0.5 * PENALTY * jump_velocity)
    return jnp.concatenate([on_pressure, on_velocity], 1)


def radial_neighbours(rad_minus, rad_plus):
    below_trace = jnp.concatenate([jnp.zeros_like(rad_plus[..., :1]), rad_plus[..., :-1]], -1)
    above_trace = jnp.concatenate([rad_minus[..., 1:], jnp.zeros_like(rad_minus[..., :1])], -1)
    return (below_trace, above_trace)


def heun_step(states, sources, neighbour_fn, bulk_modulus, inverse_size, coupling, selects):

    def rate_of(field_now):
        traces_all = jnp.einsum("ck,scr->skr", selects, field_now, precision=lax.Precision.HIGHEST)
        traces = [traces_all[:, 32 * f : 32 * f + 32] for f in range(6)]
        neighbours = neighbour_fn(traces)
        face_rates = jnp.concatenate(
            [
                face_term(traces[f], neighbours[f], bulk_modulus, inverse_size, 2.0 * (f % 2) - 1.0)
                for f in range(6)
            ],
            1,
        )
        lifted = jnp.einsum("ck,skr->scr", selects, face_rates, precision=lax.Precision.HIGHEST)
        return volume_rate(field_now, coupling, bulk_modulus, inverse_size) + lifted + sources

    first_rate = rate_of(states)
    second_rate = rate_of(states + TIME_STEP * first_rate)
    return states + 0.5 * TIME_STEP * (first_rate + second_rate)


def divergence(field_state, coupling, inverse_size):
    return -inverse_size * jnp.einsum(
        "cn,...cr->...nr", coupling[:, :64], field_state, precision=lax.Precision.HIGHEST
    )


def pressure_source(perturb, forward_div, adjoint_div):
    source_terms = jnp.concatenate(
        [perturb[:, None, :] * forward_div[None], perturb[:, None, :] * adjoint_div[None]], 0
    )
    return jnp.concatenate(
        [source_terms, jnp.zeros((source_terms.shape[0], 192, source_terms.shape[2]), jnp.float32)],
        1,
    )


def sensitivity(
    new_forward, new_adjoint, forward_div, adjoint_state, inverse_size, coupling, quadrature
):
    new_div = divergence(new_forward, coupling, inverse_size)
    integrand = new_adjoint[:, :64] * forward_div[None] + adjoint_state[None, :64] * new_div
    return jnp.einsum("n,pnr->pr", quadrature, integrand, precision=lax.Precision.HIGHEST) / (
        64.0 * inverse_size**3
    )


def reorient(neighbour, codes_face, orient):
    result = jnp.zeros_like(neighbour)
    for code in range(8):
        permuted = neighbour[:, orient[code], :]
        result = result + jnp.where((codes_face == code)[None, None, :], permuted, 0.0)
    return result


def shift_lat(rim, offset):
    return shifted(rim, "lat", offset)


def shift_lon(rim, offset):
    return from_behind(rim, "lon", offset)


def rims_lat(first_rim, last_rim):
    from_south = shift_lat(last_rim, 1)
    from_north = shift_lat(first_rim, -1)
    return (from_south, from_north)


def rims_lon(first_rim, last_rim):
    from_west = shift_lon(last_rim, 1)
    from_east = shift_lon(first_rim, -1)
    return (from_west, from_east)


def body(
    forward_state,
    adjoint_state,
    inc_forward,
    inc_adjoint,
    bulk_modulus,
    inverse_size,
    face_codes,
    block_map,
    probe_dirs,
):
    coupling, selects, orient, quadrature = node_tables()
    whole_dirs = lax.all_gather(probe_dirs, ("lat", "lon"), axis=1, tiled=True)
    perturb = jnp.take(whole_dirs, block_map, axis=1)
    forward_div = divergence(forward_state, coupling, inverse_size)
    adjoint_div = divergence(adjoint_state, coupling, inverse_size)

    def neighbour_fn(traces):
        from_south, from_north = rims_lat(traces[0], traces[1])
        from_west, from_east = rims_lon(traces[2], traces[3])
        sides = [from_south, from_north, from_west, from_east]
        horizontal = [reorient(sides[f], face_codes[f], orient) for f in range(4)]
        below_trace, above_trace = radial_neighbours(traces[4], traces[5])
        return horizontal + [below_trace, above_trace]

    probe_count = inc_forward.shape[0]
    states = jnp.concatenate([inc_forward, inc_adjoint], 0)
    sources = pressure_source(perturb, forward_div, adjoint_div)
    updated = heun_step(
        states, sources, neighbour_fn, bulk_modulus, inverse_size, coupling, selects
    )
    new_forward = updated[:probe_count]
    new_adjoint = updated[probe_count:]
    element_terms = sensitivity(
        new_forward, new_adjoint, forward_div, adjoint_state, inverse_size, coupling, quadrature
    )
    partial_sums = jax.ops.segment_sum(
        element_terms.T, block_map, num_segments=whole_dirs.shape[1]
    ).T
    hess_vec = lax.psum_scatter(partial_sums, ("lat", "lon"), scatter_dimension=1, tiled=True)
    return (new_forward, new_adjoint, hess_vec)


def solution(mesh):
    placed = (
        P(None, ("lat", "lon")),
        P(None, ("lat", "lon")),
        P(None, None, ("lat", "lon")),
        P(None, None, ("lat", "lon")),
        P(("lat", "lon")),
        P(("lat", "lon")),
        P(None, ("lat", "lon")),
        P(("lat", "lon")),
        P(None, ("lat", "lon")),
    )
    return jax.shard_map(
        body,
        mesh=mesh,
        in_specs=placed,
        out_specs=(
            P(None, None, ("lat", "lon")),
            P(None, None, ("lat", "lon")),
            P(None, ("lat", "lon")),
        ),
        check_vma=False,
    )
```

profile of v0, /device:TPU:1, one launch (start us, length us, event | category | flops | bytes accessed | tf_op | source)
XLA Modules:
  0.0 863.0 jit_solution(8838339508929728169)
XLA Ops:
  4.5 7.4 collective-permute-start.3
  11.9 3.0 collective-permute-start.1
  14.9 3.1 collective-permute-start
  21.9 597.1 %all-gather = f32[256,1,4]{2,1,0:T(1,128)S(1)} all-gather(f32[1,1,4]{2,1,0:T(1,128)S(1)} %bitcast.171), channel_id=1, replica_groups=mesh['lat'=16,'lon'=16] {'lat','lon'}, dimensions={0}, use_global_device_ids=true | all-gather | bytes 4112 | tf_op jit(solution)/shard_map/all_gather | solution.py:191
  622.4 2.1 fusion.7
  627.0 1.2 gather_fusion.24
  628.3 1.2 gather_fusion.25
  631.7 1.2 gather_fusion.17
  633.0 1.3 gather_fusion.26
  634.2 1.2 gather_fusion.18
  635.5 1.2 gather_fusion.27
  636.7 1.2 gather_fusion.19
  637.9 1.2 gather_fusion.28
  639.2 1.3 gather_fusion.20
  642.9 1.3 gather_fusion.30
  644.1 1.2 gather_fusion.22
  646.6 1.2 gather_fusion.23
  649.4 1.2 gather_fusion.9
  650.7 1.2 gather_fusion.10
  651.9 1.3 gather_fusion.11
  653.2 1.2 gather_fusion.12
  654.4 1.3 gather_fusion.13
  655.6 1.2 gather_fusion.14
  656.9 1.2 gather_fusion.15
  659.1 1.2 gather_fusion
  660.3 1.2 gather_fusion.1
  661.6 1.2 gather_fusion.2
  664.1 1.2 gather_fusion.4
  666.5 1.2 gather_fusion.6
  667.8 1.2 gather_fusion.7
  669.7 1.5 bitcast_add_fusion.7
  680.6 2.2 fusion.8
  683.5 1.5 collective-permute-start.6
  684.9 33.6 %collective-permute-start.5 = (f32[8,32,128]{2,1,0:T(8,128)}, f32[8,32,128]{2,1,0:T(8,128)}, u32[]{:S(2)}, u32[]{:S(2)}) collective-permute-start(f32[8,32,128]{2,1,0:T(8,128)} %get-tuple-element.18), channel_id=1, source_target_pairs={{16,0},{32,16},{48,32},{64,48},{80,64},{96,80},{112,96},{128,112},... | collective-permute-start | bytes 393224 | tf_op jit(solution)/shard_map/ppermute | solution.py:15
  718.6 2.1 collective-permute-start.4
  723.9 1.2 gather_fusion.59
  725.2 1.2 gather_fusion.60
  726.4 1.2 gather_fusion.61
  727.6 1.3 gather_fusion.62
  728.9 1.2 gather_fusion.63
  732.4 1.2 gather_fusion.49
  733.6 1.3 gather_fusion.50
  734.8 1.2 gather_fusion.51
  736.1 1.2 gather_fusion.52
  738.6 1.3 gather_fusion.54
  739.8 1.2 gather_fusion.55
  741.0 1.3 gather_fusion.56
  743.3 1.2 gather_fusion.41
  744.5 1.2 gather_fusion.42
  745.8 1.2 gather_fusion.43
  747.0 1.2 gather_fusion.44
  749.5 1.2 gather_fusion.46
  750.7 1.2 gather_fusion.47
  752.0 1.2 gather_fusion.48
  754.2 1.2 gather_fusion.33
  755.4 1.2 gather_fusion.34
  757.9 1.2 gather_fusion.36
  760.4 1.2 gather_fusion.38
  761.6 1.2 gather_fusion.39
  762.8 1.2 gather_fusion.40
  764.2 1.6 bitcast_add_fusion.3
  772.1 1.3 fusion.4
  776.1 1.2 scatter_custom_fusion
  777.4 85.2 %all-reduce.5 = f32[4,256]{0,1:T(8,128)S(1)} all-reduce(f32[4,256]{0,1:T(8,128)S(1)} %bitcast.169), channel_id=2, replica_groups=mesh['lat'=16,'lon'=16] {'lat','lon'}, use_global_device_ids=true, to_apply=%region_1.2.clone | all-reduce | flops 1024 | bytes 8192
  (375 shorter events, 55.7 us)
Async XLA Ops:
  0.6 20.0 %copy-start = (f32[256,128]{1,0:T(8,128)S(1)}, f32[256,128]{1,0:T(8,128)}, u32[]{:S(2)}) copy-start(f32[256,128]{1,0:T(8,128)} %param.140) | copy-start | bytes 393220
  0.6 1.2 copy-start.61
  4.5 621.5 %collective-permute-start.3 = (f32[8,32,128]{2,1,0:T(8,128)}, f32[8,32,128]{2,1,0:T(8,128)}, u32[]{:S(2)}, u32[]{:S(2)}) collective-permute-start(f32[8,32,128]{2,1,0:T(8,128)} %get-tuple-element.22), channel_id=1, source_target_pairs={{0,15},{1,0},{2,1},{3,2},{4,3},{5,4},{6,5},{7,6},{8,7},{9,8},{10,9... | collective-permute-start | bytes 393224 | tf_op jit(solution)/shard_map/ppermute | solution.py:21
  11.9 6.1 copy-start.71
  11.9 617.6 %collective-permute-start.2 = (f32[8,32,128]{2,1,0:T(8,128)}, f32[8,32,128]{2,1,0:T(8,128)}, u32[]{:S(2)}, u32[]{:S(2)}) collective-permute-start(f32[8,32,128]{2,1,0:T(8,128)} %get-tuple-element.23), channel_id=1, source_target_pairs={{0,1},{1,2},{2,3},{3,4},{4,5},{5,6},{6,7},{7,8},{8,9},{9,10},{10,1... | collective-permute-start | bytes 393224 | tf_op jit(solution)/shard_map/ppermute | solution.py:21
  11.9 636.0 %collective-permute-start.1 = (f32[8,32,128]{2,1,0:T(8,128)}, f32[8,32,128]{2,1,0:T(8,128)}, u32[]{:S(2)}, u32[]{:S(2)}) collective-permute-start(f32[8,32,128]{2,1,0:T(8,128)} %get-tuple-element.24), channel_id=1, source_target_pairs={{16,0},{32,16},{48,32},{64,48},{80,64},{96,80},{112,96},{128,112},... | collective-permute-start | bytes 393224 | tf_op jit(solution)/shard_map/ppermute | solution.py:15
  14.9 643.3 %collective-permute-start = (f32[8,32,128]{2,1,0:T(8,128)}, f32[8,32,128]{2,1,0:T(8,128)}, u32[]{:S(2)}, u32[]{:S(2)}) collective-permute-start(f32[8,32,128]{2,1,0:T(8,128)} %get-tuple-element.25), channel_id=1, source_target_pairs={{0,16},{16,32},{32,48},{48,64},{64,80},{80,96},{96,112},{112,128},... | collective-permute-start | bytes 393224 | tf_op jit(solution)/shard_map/ppermute | solution.py:15
  19.3 1.3 copy-start.62
  20.6 601.7 %copy-start.68 = (f32[128]{0:T(128)}, f32[128]{0:T(128)S(1)}, u32[]{:S(2)}) copy-start(f32[128]{0:T(128)S(1)} %get-tuple-element.61) | copy-start | bytes 1540
  622.4 2.1 copy-start.3
  622.4 2.1 copy-start.70
  631.7 1.2 copy-start.67
  634.2 1.2 copy-start.66
  669.7 1.7 copy-start.59
  669.7 1.7 copy-start.60
  671.3 1.0 copy-start.54
  671.3 1.1 copy-start.55
  671.3 1.1 copy-start.109
  671.3 1.1 copy-start.111
  671.3 1.1 copy-start.113
  671.3 1.1 copy-start.115
  671.3 1.1 copy-start.117
  672.8 1.1 copy-start.39
  672.8 1.1 copy-start.93
  672.8 1.1 copy-start.95
  672.8 1.1 copy-start.97
  674.2 1.1 copy-start.23
  674.2 1.1 copy-start.77
  674.2 1.1 copy-start.79
  674.2 1.1 copy-start.81
  683.5 37.9 %collective-permute-start.7 = (f32[8,32,128]{2,1,0:T(8,128)S(1)}, f32[8,32,128]{2,1,0:T(8,128)S(1)}, u32[]{:S(2)}, u32[]{:S(2)}) collective-permute-start(f32[8,32,128]{2,1,0:T(8,128)S(1)} %get-tuple-element.16), channel_id=1, source_target_pairs={{0,15},{1,0},{2,1},{3,2},{4,3},{5,4},{6,5},{7,6},{8,7},{9,8},{10,9... | collective-permute-start | bytes 393224 | tf_op jit(solution)/shard_map/ppermute | solution.py:21
  683.5 47.9 %collective-permute-start.6 = (f32[8,32,128]{2,1,0:T(8,128)}, f32[8,32,128]{2,1,0:T(8,128)}, u32[]{:S(2)}, u32[]{:S(2)}) collective-permute-start(f32[8,32,128]{2,1,0:T(8,128)} %get-tuple-element.17), channel_id=1, source_target_pairs={{0,1},{1,2},{2,3},{3,4},{4,5},{5,6},{6,7},{7,8},{8,9},{9,10},{10,1... | collective-permute-start | bytes 393224 | tf_op jit(solution)/shard_map/ppermute | solution.py:21
  684.9 57.4 %collective-permute-start.5 = (f32[8,32,128]{2,1,0:T(8,128)}, f32[8,32,128]{2,1,0:T(8,128)}, u32[]{:S(2)}, u32[]{:S(2)}) collective-permute-start(f32[8,32,128]{2,1,0:T(8,128)} %get-tuple-element.18), channel_id=1, source_target_pairs={{16,0},{32,16},{48,32},{64,48},{80,64},{96,80},{112,96},{128,112},... | collective-permute-start | bytes 393224 | tf_op jit(solution)/shard_map/ppermute | solution.py:15
  718.6 34.6 %collective-permute-start.4 = (f32[8,32,128]{2,1,0:T(8,128)}, f32[8,32,128]{2,1,0:T(8,128)}, u32[]{:S(2)}, u32[]{:S(2)}) collective-permute-start(f32[8,32,128]{2,1,0:T(8,128)} %get-tuple-element.19), channel_id=1, source_target_pairs={{0,16},{16,32},{32,48},{48,64},{64,80},{80,96},{96,112},{112,128},... | collective-permute-start | bytes 393224 | tf_op jit(solution)/shard_map/ppermute | solution.py:15
  721.4 49.6 %copy-start.11 = (f32[8,32,127]{2,1,0:T(8,128)}, f32[8,32,127]{2,1,0:T(8,128)S(1)}, u32[]{:S(2)}) copy-start(f32[8,32,127]{2,1,0:T(8,128)S(1)} %get-tuple-element.14) | copy-start | bytes 390148
  762.8 1.3 copy-start.120
  762.8 1.3 copy-start.122
  762.8 1.3 copy-start.124
  762.8 1.3 copy-start.125
  764.1 1.8 copy-start.51
  764.1 1.8 copy-start.52
  764.1 1.8 copy-start.53
  764.1 1.8 copy-start.110
  764.1 1.8 copy-start.112
  764.1 1.8 copy-start.114
  764.2 1.8 copy-start.116
  764.2 1.8 copy-start.118
  765.8 1.1 copy-start.47
  765.9 1.1 copy-start.104
  765.9 1.1 copy-start.106
  765.9 1.1 copy-start.108
  767.3 1.1 copy-start.25
  767.3 1.1 copy-start.88
  767.3 1.1 copy-start.90
  767.3 1.1 copy-start.92
  768.7 1.1 copy-start.15
  768.7 1.1 copy-start.74
  768.8 1.1 copy-start.76
  768.8 1.1 copy-start.78
  770.0 1.9 copy-start.1
  771.0 1.1 copy-start.8
  773.4 1.1 slice-start
  773.4 1.1 copy-start.64
  773.4 1.1 copy-start.69
  (84 other events, 78.5 us)
where the time goes:
time: 864 us; the launch traced here: 863 us
  blocking collectives  682 us (79%)
  local copies, waits for them, and re-layouts  107 us (12%)
  starting transfers between devices  50.7 us (6%)
  other arithmetic  11.3 us (1%)
  matrix products  9.57 us (1%)
    all_gather x1, blocking collectives, body(): whole_dirs = lax.all_gather(probe_dirs, ('lat', 'lon'), axis=1, tiled=True)  597 us
    unnamed x1, blocking collectives  85.2 us
    gather x64, local copies, waits for them, and re-layouts, reorient(): permuted = neighbour[:, orient[code], :]  78.6 us
    ppermute x4, starting transfers between devices, shifted(): return lax.ppermute(block, axis, route)  41.9 us
  transfers between devices with their start and end apart: 8, of which 0 were waited for; matrix products, arithmetic and copies ran while one was open for 8% of the time, Pallas kernels for 0%

commit v1 on v0

--- a/solution.py
+++ b/solution.py
@@ -188,7 +188,12 @@
     probe_dirs,
 ):
     coupling, selects, orient, quadrature = node_tables()
-    whole_dirs = lax.all_gather(probe_dirs, ("lat", "lon"), axis=1, tiled=True)
+    whole_dirs = jnp.concatenate(
+        lax.all_to_all(
+            jnp.stack([probe_dirs] * lax.axis_size(("lat", "lon"))), ("lat", "lon"), 0, 0
+        ),
+        axis=1,
+    )
     perturb = jnp.take(whole_dirs, block_map, axis=1)
     forward_div = divergence(forward_state, coupling, inverse_size)
     adjoint_div = divergence(adjoint_state, coupling, inverse_size)

time: 864 us -> 257 us (0.30)
  blocking collectives: 682 us -> 83.4 us
  starting transfers between devices: 50.7 us -> 38.5 us
    all_gather x1 -> x0, blocking collectives: 597 us -> none  [body(): whole_dirs = lax.all_gather(probe_dirs, ('lat', 'lon'), axis=1, tiled=True)]
    ppermute x4, starting transfers between devices: 41.9 us -> 11.8 us  [shifted(): return lax.ppermute(block, axis, route)]
    all_to_all x0 -> x1, starting transfers between devices: none -> 16.7 us  [body(): lax.all_to_all(jnp.stack([probe_dirs] * lax.axis_size(('lat', 'lon'))), (...]
  transfers between devices with their start and end apart: 8 -> 9, of which waited for: 0 -> 1; matrix products, arithmetic and copies ran while one was open for 8% -> 29% of each run, Pallas kernels for 0% -> 0%
where the time goes in v1:
time: 257 us; the launch traced here: 256 us
  local copies, waits for them, and re-layouts  106 us (41%)
  blocking collectives  83.4 us (32%)
  starting transfers between devices  38.5 us (15%)
  other arithmetic  13.7 us (5%)
  matrix products  8.59 us (3%)
  waiting for transfers between devices  3.37 us (1%)
    unnamed x1, blocking collectives  83.4 us
    gather x64, local copies, waits for them, and re-layouts, reorient(): permuted = neighbour[:, orient[code], :]  78.3 us
    all_to_all x1, starting transfers between devices, body(): lax.all_to_all(jnp.stack([probe_dirs] * lax.axis_size(('lat', 'lon'))), (...  16.7 us
    unnamed x290, local copies, waits for them, and re-layouts  14.5 us
    ppermute x4, starting transfers between devices, shifted(): return lax.ppermute(block, axis, route)  11.8 us
    ppermute x4, starting transfers between devices, from_behind(): return lax.ppermute(value, axis, pairs)  10 us
  transfers between devices with their start and end apart: 9, of which 1 were waited for; matrix products, arithmetic and copies ran while one was open for 29% of the time, Pallas kernels for 0%

profile of v1, /device:TPU:1, one launch (start us, length us, event | category | flops | bytes accessed | tf_op | source)
XLA Modules:
  0.0 256.2 jit_solution(18142124840605071247)
XLA Ops:
  4.5 7.4 %collective-permute-start.3 = (f32[8,32,128]{2,1,0:T(8,128)}, f32[8,32,128]{2,1,0:T(8,128)}, u32[]{:S(2)}, u32[]{:S(2)}) collective-permute-start(f32[8,32,128]{2,1,0:T(8,128)} %get-tuple-element.22), channel_id=1, source_target_pairs={{0,15},{1,0},{2,1},{3,2},{4,3},{5,4},{6,5},{7,6},{8,7},{9,8},{10,9... | collective-permute-start | bytes 393224 | tf_op jit(solution)/shard_map/ppermute | solution.py:21
  11.9 2.9 %collective-permute-start.1 = (f32[8,32,128]{2,1,0:T(8,128)}, f32[8,32,128]{2,1,0:T(8,128)}, u32[]{:S(2)}, u32[]{:S(2)}) collective-permute-start(f32[8,32,128]{2,1,0:T(8,128)} %get-tuple-element.24), channel_id=1, source_target_pairs={{16,0},{32,16},{48,32},{64,48},{80,64},{96,80},{112,96},{128,112},... | collective-permute-start | bytes 393224 | tf_op jit(solution)/shard_map/ppermute | solution.py:15
  14.7 3.1 %collective-permute-start = (f32[8,32,128]{2,1,0:T(8,128)}, f32[8,32,128]{2,1,0:T(8,128)}, u32[]{:S(2)}, u32[]{:S(2)}) collective-permute-start(f32[8,32,128]{2,1,0:T(8,128)} %get-tuple-element.25), channel_id=1, source_target_pairs={{0,16},{16,32},{32,48},{48,64},{64,80},{80,96},{96,112},{112,128},... | collective-permute-start | bytes 393224 | tf_op jit(solution)/shard_map/ppermute | solution.py:15
  18.6 16.7 %all-to-all-start = ((f32[256,4,1]{1,2,0:T(1,128)}), f32[256,4,1]{1,2,0:T(1,128)}, u32[]{:S(2)}, u32[]{:S(2)}) async-start(f32[256,4,1]{1,2,0:T(1,128)} %stack.2), calls=%async_computation | async-start | bytes 262144 | tf_op jit(solution)/shard_map/all_to_all | solution.py:192
  44.1 3.3 %all-to-all-done = f32[256,4,1]{1,2,0:T(1,128)} async-done(((f32[256,4,1]{1,2,0:T(1,128)}), f32[256,4,1]{1,2,0:T(1,128)}, u32[]{:S(2)}, u32[]{:S(2)}) %all-to-all-start) | async-done | bytes 4128 | tf_op jit(solution)/shard_map/all_to_all | solution.py:192
  47.5 1.7 gather_fusion.32
  51.1 1.2 gather_fusion.24
  52.3 1.2 gather_fusion.25
  54.5 1.2 gather_fusion.16
  55.8 1.2 gather_fusion.17
  57.0 1.2 gather_fusion.26
  59.5 1.2 gather_fusion.27
  60.7 1.2 gather_fusion.19
  61.9 1.2 gather_fusion.28
  63.2 1.2 gather_fusion.20
  64.4 1.2 gather_fusion.29
  65.7 1.2 gather_fusion.21
  68.1 1.2 gather_fusion.22
  69.4 1.2 gather_fusion.31
  70.6 1.2 gather_fusion.23
  73.4 1.2 gather_fusion.9
  75.9 1.2 gather_fusion.11
  77.1 1.2 gather_fusion.12
  78.4 1.2 gather_fusion.13
  80.8 1.2 gather_fusion.15
  84.3 1.2 gather_fusion.1
  86.7 1.2 gather_fusion.3
  88.0 1.2 gather_fusion.4
  90.4 1.2 gather_fusion.6
  91.7 1.2 gather_fusion.7
  93.6 1.5 bitcast_add_fusion.7
  104.5 2.2 fusion.8
  107.3 2.6 %collective-permute-start.7 = (f32[8,32,128]{2,1,0:T(8,128)S(1)}, f32[8,32,128]{2,1,0:T(8,128)S(1)}, u32[]{:S(2)}, u32[]{:S(2)}) collective-permute-start(f32[8,32,128]{2,1,0:T(8,128)S(1)} %get-tuple-element.16), channel_id=1, source_target_pairs={{0,15},{1,0},{2,1},{3,2},{4,3},{5,4},{6,5},{7,6},{8,7},{9,8},{10,9... | collective-permute-start | bytes 393224 | tf_op jit(solution)/shard_map/ppermute | solution.py:21
  110.0 2.6 %collective-permute-start.5 = (f32[8,32,128]{2,1,0:T(8,128)}, f32[8,32,128]{2,1,0:T(8,128)}, u32[]{:S(2)}, u32[]{:S(2)}) collective-permute-start(f32[8,32,128]{2,1,0:T(8,128)} %get-tuple-element.18), channel_id=1, source_target_pairs={{16,0},{32,16},{48,32},{64,48},{80,64},{96,80},{112,96},{128,112},... | collective-permute-start | bytes 393224 | tf_op jit(solution)/shard_map/ppermute | solution.py:15
  112.6 3.3 %collective-permute-start.4 = (f32[8,32,128]{2,1,0:T(8,128)}, f32[8,32,128]{2,1,0:T(8,128)}, u32[]{:S(2)}, u32[]{:S(2)}) collective-permute-start(f32[8,32,128]{2,1,0:T(8,128)} %get-tuple-element.19), channel_id=1, source_target_pairs={{0,16},{16,32},{32,48},{48,64},{64,80},{80,96},{96,112},{112,128},... | collective-permute-start | bytes 393224 | tf_op jit(solution)/shard_map/ppermute | solution.py:15
  116.6 1.2 gather_fusion.57
  117.8 1.2 gather_fusion.58
  120.3 1.2 gather_fusion.60
  121.5 1.2 gather_fusion.61
  122.8 1.2 gather_fusion.62
  124.0 1.2 gather_fusion.63
  125.3 1.2 gather_fusion.64
  127.5 1.2 gather_fusion.49
  129.9 1.2 gather_fusion.51
  131.2 1.2 gather_fusion.52
  132.4 1.2 gather_fusion.53
  133.6 1.2 gather_fusion.54
  134.9 1.2 gather_fusion.55
  136.1 1.2 gather_fusion.56
  139.6 1.2 gather_fusion.42
  140.8 1.2 gather_fusion.43
  143.3 1.2 gather_fusion.45
  147.0 1.2 gather_fusion.48
  149.2 1.2 gather_fusion.33
  150.4 1.2 gather_fusion.34
  151.7 1.2 gather_fusion.35
  152.9 1.2 gather_fusion.36
  154.1 1.2 gather_fusion.37
  156.6 1.2 gather_fusion.39
  157.8 1.2 gather_fusion.40
  159.2 1.6 bitcast_add_fusion.3
  167.1 1.3 fusion.4
  171.1 1.2 scatter_custom_fusion
  172.3 83.4 %all-reduce.5 = f32[4,256]{0,1:T(8,128)S(1)} all-reduce(f32[4,256]{0,1:T(8,128)S(1)} %bitcast.171), channel_id=2, replica_groups=mesh['lat'=16,'lon'=16] {'lat','lon'}, use_global_device_ids=true, to_apply=%region_1.2.clone | all-reduce | flops 1024 | bytes 8192
  (387 shorter events, 58.6 us)
Async XLA Ops:
  0.6 37.9 %copy-start = (f32[256,128]{1,0:T(8,128)S(1)}, f32[256,128]{1,0:T(8,128)}, u32[]{:S(2)}) copy-start(f32[256,128]{1,0:T(8,128)} %param.140) | copy-start | bytes 393220
  0.6 1.2 copy-start.62
  4.5 45.6 %collective-permute-start.3 = (f32[8,32,128]{2,1,0:T(8,128)}, f32[8,32,128]{2,1,0:T(8,128)}, u32[]{:S(2)}, u32[]{:S(2)}) collective-permute-start(f32[8,32,128]{2,1,0:T(8,128)} %get-tuple-element.22), channel_id=1, source_target_pairs={{0,15},{1,0},{2,1},{3,2},{4,3},{5,4},{6,5},{7,6},{8,7},{9,8},{10,9... | collective-permute-start | bytes 393224 | tf_op jit(solution)/shard_map/ppermute | solution.py:21
  11.9 41.7 %collective-permute-start.2 = (f32[8,32,128]{2,1,0:T(8,128)}, f32[8,32,128]{2,1,0:T(8,128)}, u32[]{:S(2)}, u32[]{:S(2)}) collective-permute-start(f32[8,32,128]{2,1,0:T(8,128)} %get-tuple-element.23), channel_id=1, source_target_pairs={{0,1},{1,2},{2,3},{3,4},{4,5},{5,6},{6,7},{7,8},{8,9},{9,10},{10,1... | collective-permute-start | bytes 393224 | tf_op jit(solution)/shard_map/ppermute | solution.py:21
  11.9 60.0 %collective-permute-start.1 = (f32[8,32,128]{2,1,0:T(8,128)}, f32[8,32,128]{2,1,0:T(8,128)}, u32[]{:S(2)}, u32[]{:S(2)}) collective-permute-start(f32[8,32,128]{2,1,0:T(8,128)} %get-tuple-element.24), channel_id=1, source_target_pairs={{16,0},{32,16},{48,32},{64,48},{80,64},{96,80},{112,96},{128,112},... | collective-permute-start | bytes 393224 | tf_op jit(solution)/shard_map/ppermute | solution.py:15
  14.7 3.1 %copy-start.131 = (f32[4,1]{0,1:T(1,128)S(1)}, f32[4,1]{0,1:T(1,128)}, u32[]{:S(2)}) copy-start(f32[4,1]{0,1:T(1,128)} %param.148) | copy-start | bytes 52
  14.7 67.3 %collective-permute-start = (f32[8,32,128]{2,1,0:T(8,128)}, f32[8,32,128]{2,1,0:T(8,128)}, u32[]{:S(2)}, u32[]{:S(2)}) collective-permute-start(f32[8,32,128]{2,1,0:T(8,128)} %get-tuple-element.25), channel_id=1, source_target_pairs={{0,16},{16,32},{32,48},{48,64},{64,80},{80,96},{96,112},{112,128},... | collective-permute-start | bytes 393224 | tf_op jit(solution)/shard_map/ppermute | solution.py:15
  18.6 16.7 %copy-start.75 = (s32[4,128]{1,0:T(4,128)S(1)}, s32[4,128]{1,0:T(4,128)}, u32[]{:S(2)}) copy-start(s32[4,128]{1,0:T(4,128)} %param.146) | copy-start | bytes 6148
  18.6 28.9 %all-to-all-start = ((f32[256,4,1]{1,2,0:T(1,128)}), f32[256,4,1]{1,2,0:T(1,128)}, u32[]{:S(2)}, u32[]{:S(2)}) async-start(f32[256,4,1]{1,2,0:T(1,128)} %stack.2), calls=%async_computation | async-start | bytes 262144 | tf_op jit(solution)/shard_map/all_to_all | solution.py:192
  36.6 1.4 copy-start.141
  36.6 1.4 copy-start.142
  36.6 1.9 copy-start.63
  37.4 1.4 copy-start.64
  38.5 3.8 %copy-start.73 = (f32[128]{0:T(128)}, f32[128]{0:T(128)S(1)}, u32[]{:S(2)}) copy-start(f32[128]{0:T(128)S(1)} %get-tuple-element.61) | copy-start | bytes 1540
  38.5 3.9 %copy-start.13 = (f32[256,256,1]{1,0,2:T(8,128)S(1)}, f32[256,256,1]{1,0,2:T(8,128)}, u32[]{:S(2)}) copy-start(f32[256,256,1]{1,0,2:T(8,128)} %constant.176) | copy-start | bytes 786436
  42.4 1.1 copy-start.3
  47.5 1.7 copy-start.133
  55.8 1.2 copy-start.68
  58.2 1.2 copy-start.67
  60.7 1.2 copy-start.70
  63.2 1.2 copy-start.69
  65.7 1.2 copy-start.72
  68.1 1.2 copy-start.71
  93.6 1.7 copy-start.60
  93.6 1.7 copy-start.61
  95.2 1.1 copy-start.56
  95.2 1.1 copy-start.113
  95.2 1.1 copy-start.115
  95.2 1.1 copy-start.117
  95.2 1.1 copy-start.119
  95.2 1.1 copy-start.121
  96.7 1.1 copy-start.40
  96.7 1.1 copy-start.97
  98.1 1.1 copy-start.24
  98.1 1.1 copy-start.81
  107.3 9.2 %collective-permute-start.7 = (f32[8,32,128]{2,1,0:T(8,128)S(1)}, f32[8,32,128]{2,1,0:T(8,128)S(1)}, u32[]{:S(2)}, u32[]{:S(2)}) collective-permute-start(f32[8,32,128]{2,1,0:T(8,128)S(1)} %get-tuple-element.16), channel_id=1, source_target_pairs={{0,15},{1,0},{2,1},{3,2},{4,3},{5,4},{6,5},{7,6},{8,7},{9,8},{10,9... | collective-permute-start | bytes 393224 | tf_op jit(solution)/shard_map/ppermute | solution.py:21
  110.0 16.5 %collective-permute-start.6 = (f32[8,32,128]{2,1,0:T(8,128)}, f32[8,32,128]{2,1,0:T(8,128)}, u32[]{:S(2)}, u32[]{:S(2)}) collective-permute-start(f32[8,32,128]{2,1,0:T(8,128)} %get-tuple-element.17), channel_id=1, source_target_pairs={{0,1},{1,2},{2,3},{3,4},{4,5},{5,6},{6,7},{7,8},{8,9},{9,10},{10,1... | collective-permute-start | bytes 393224 | tf_op jit(solution)/shard_map/ppermute | solution.py:21
  110.0 27.4 %collective-permute-start.5 = (f32[8,32,128]{2,1,0:T(8,128)}, f32[8,32,128]{2,1,0:T(8,128)}, u32[]{:S(2)}, u32[]{:S(2)}) collective-permute-start(f32[8,32,128]{2,1,0:T(8,128)} %get-tuple-element.18), channel_id=1, source_target_pairs={{16,0},{32,16},{48,32},{64,48},{80,64},{96,80},{112,96},{128,112},... | collective-permute-start | bytes 393224 | tf_op jit(solution)/shard_map/ppermute | solution.py:15
  112.6 35.6 %collective-permute-start.4 = (f32[8,32,128]{2,1,0:T(8,128)}, f32[8,32,128]{2,1,0:T(8,128)}, u32[]{:S(2)}, u32[]{:S(2)}) collective-permute-start(f32[8,32,128]{2,1,0:T(8,128)} %get-tuple-element.19), channel_id=1, source_target_pairs={{0,16},{16,32},{32,48},{48,64},{64,80},{80,96},{96,112},{112,128},... | collective-permute-start | bytes 393224 | tf_op jit(solution)/shard_map/ppermute | solution.py:15
  116.5 49.4 %copy-start.11 = (f32[8,32,127]{2,1,0:T(8,128)}, f32[8,32,127]{2,1,0:T(8,128)S(1)}, u32[]{:S(2)}) copy-start(f32[8,32,127]{2,1,0:T(8,128)S(1)} %get-tuple-element.14) | copy-start | bytes 390148
  157.8 1.3 copy-start.124
  157.8 1.3 copy-start.126
  157.8 1.3 copy-start.128
  157.8 1.3 copy-start.129
  159.1 1.8 copy-start.52
  159.1 1.8 copy-start.53
  159.1 1.8 copy-start.54
  159.1 1.8 copy-start.114
  159.1 1.8 copy-start.116
  159.1 1.8 copy-start.118
  159.2 1.8 copy-start.120
  159.2 1.8 copy-start.122
  160.8 1.1 copy-start.48
  160.9 1.1 copy-start.108
  160.9 1.1 copy-start.110
  160.9 1.1 copy-start.112
  162.3 1.1 copy-start.26
  162.3 1.1 copy-start.92
  163.7 1.1 copy-start.16
  163.7 1.1 copy-start.78
  165.0 1.9 copy-start.1
  166.0 1.1 copy-start.8
  168.4 1.1 slice-start
  168.4 1.1 copy-start.65
  (90 other events, 85.6 us)
